TPU v7x, 256 devices: a whole 4x4x8 slice. The times are simulated.
256 devices in a mesh: ctx: 64 (over x, z, core), tp: 4 (over y).
Axes of the slice: x: 4, y: 4, z: 8, core: 2. Of those that a mesh axis runs over, the one named last changes fastest.
Arguments:
- inputs: bfloat16 [8192, 4096], P('ctx'), may hold values from -6 to 6
- w_query: bfloat16 [4096, 4096], P(None, 'tp'), may hold values from -0.109375 to 0.109375
- w_key: bfloat16 [4096, 512], P(None, 'tp'), may hold values from -0.109375 to 0.109375
- w_value: bfloat16 [4096, 512], P(None, 'tp'), may hold values from -0.09375 to 0.09375
- attn_out: bfloat16 [8192, 4096], P('ctx', 'tp'), may hold values from -6 to 6
- d_out: bfloat16 [8192, 4096], P('ctx', 'tp'), may hold values from -6 to 6
- block_order: int32 [128], replicated, may hold values from 0 to 127, each once
Outputs:
- d_input: bfloat16 [8192, 4096], P('ctx', 'tp')
Inputs may be any that keep to these rules, and one draw needn't show every extreme that they name: `block_order`: a permutation of the sequence blocks.
All inputs are finite; a program needn't handle non-finite values.
Results may differ from a plain program's by a relative error of at most 0.012.
Values may be sent and summed in bfloat16 or wider, within the bound.
No kernel may reach another device: no remote copies, remote signals or barrier semaphores. Data moves between devices by JAX's collectives and lax.ppermute only.
A program may use at most 192 MiB of HBM per device.

v0:
```python
import math
import jax
import jax.numpy as jnp
from jax import lax
from jax.sharding import PartitionSpec as P

big_negative = -1e30


def row_positions(order, start, count, span):
    rows = start + lax.iota(jnp.int32, count)
    slot = rows // span
    table = jnp.sum(
        jnp.where(slot[:, None] == lax.iota(jnp.int32, order.shape[0])[None, :], order[None, :], 0),
        axis=1,
    )
    return table * span + rows % span


def contract_rows(left, weight):
    return lax.dot_general(
        left, weight, (((1,), (1,)), ((), ())), preferred_element_type=jnp.float32
    )


def on_device(inputs, w_query, w_key, w_value, attn_out, d_out, block_order):
    tokens = inputs.shape[0]
    span = tokens // 2
    head_dim = w_key.shape[1]
    heads = w_query.shape[1] // head_dim
    scale = head_dim ** (-0.5)
    keys = jnp.dot(inputs, w_key, preferred_element_type=jnp.float32).astype(jnp.bfloat16)
    values = jnp.dot(inputs, w_value, preferred_element_type=jnp.float32).astype(jnp.bfloat16)
    seq = tokens * lax.axis_size("ctx")
    my_pos = row_positions(block_order, lax.axis_index("ctx") * tokens, tokens, span)
    latest = jnp.max(my_pos)
    queries = (
        jnp.dot(inputs, w_query, preferred_element_type=jnp.float32)
        .astype(jnp.bfloat16)
        .reshape(tokens, heads, head_dim)
    )
    grads3 = d_out.reshape(tokens, heads, head_dim)
    delta = jnp.sum(
        grads3.astype(jnp.float32) * attn_out.reshape(tokens, heads, head_dim).astype(jnp.float32),
        axis=-1,
    ).T

    def guarded(work, carry, piece_k, start):
        key_pos = row_positions(block_order, start, piece_k.shape[0], span)
        return lax.cond(jnp.min(key_pos) > latest, lambda c: c, lambda c: work(c, key_pos), carry)

    def stats_step(carry, piece_k, start):

        def work(state, key_pos):
            top, total = state
            mask = (key_pos[None, :] <= my_pos[:, None])[None]
            s = (
                jnp.einsum("thd,nd->htn", queries, piece_k, preferred_element_type=jnp.float32)
                * scale
            )
            s = jnp.where(mask, s, big_negative)
            top_new = jnp.maximum(top, jnp.max(s, axis=-1))
            terms = jnp.where(mask, jnp.exp(s - top_new[..., None]), 0.0)
            return (top_new, total * jnp.exp(top - top_new) + jnp.sum(terms, axis=-1))

        return guarded(work, carry, piece_k, start)

    def grad_step(carry, pieces, start):
        piece_k, piece_v = pieces

        def work(state, key_pos):
            dq, dk_full, dv_full = state
            mask = (key_pos[None, :] <= my_pos[:, None])[None]
            s = (
                jnp.einsum("thd,nd->htn", queries, piece_k, preferred_element_type=jnp.float32)
                * scale
            )
            p = jnp.where(mask, jnp.exp(s - lse[..., None]), 0.0)
            dp = jnp.einsum("thd,nd->htn", grads3, piece_v, preferred_element_type=jnp.float32)
            ds_b = (p * (dp - delta[..., None]) * scale).astype(jnp.bfloat16)
            p_b = p.astype(jnp.bfloat16)
            dq = dq + jnp.einsum("htn,nd->thd", ds_b, piece_k, preferred_element_type=jnp.float32)
            dk_piece = jnp.einsum("htn,thd->nd", ds_b, queries, preferred_element_type=jnp.float32)
            dv_piece = jnp.einsum("htn,thd->nd", p_b, grads3, preferred_element_type=jnp.float32)
            dk_full = lax.dynamic_update_slice_in_dim(dk_full, dk_piece, start, 0)
            dv_full = lax.dynamic_update_slice_in_dim(dv_full, dv_piece, start, 0)
            return (dq, dk_full, dv_full)

        return guarded(work, carry, piece_k, start)

    stats_init = (
        jnp.full((heads, tokens), big_negative, jnp.float32),
        jnp.zeros((heads, tokens), jnp.float32),
    )
    zero_rows = jnp.zeros((seq, head_dim), jnp.float32)
    grad_init = (jnp.zeros((tokens, heads, head_dim), jnp.float32), zero_rows, zero_rows)
    all_keys, all_values = (
        lax.all_gather(keys, "ctx", axis=0, tiled=True),
        lax.all_gather(values, "ctx", axis=0, tiled=True),
    )
    block = math.gcd(seq, 1024)
    count = seq // block

    def stats_loop(i, state):
        start = (i * block).astype(jnp.int32)
        return stats_step(state, lax.dynamic_slice_in_dim(all_keys, start, block, 0), start)

    top, total = lax.fori_loop(0, count, stats_loop, stats_init)
    lse = top + jnp.log(total)

    def grad_loop(i, state):
        start = (i * block).astype(jnp.int32)
        pieces = (
            lax.dynamic_slice_in_dim(all_keys, start, block, 0),
            lax.dynamic_slice_in_dim(all_values, start, block, 0),
        )
        return grad_step(state, pieces, start)

    dq, dk_full, dv_full = lax.fori_loop(0, count, grad_loop, grad_init)
    dk_mine, dv_mine = (
        lax.psum_scatter(dk_full, "ctx", scatter_dimension=0, tiled=True),
        lax.psum_scatter(dv_full, "ctx", scatter_dimension=0, tiled=True),
    )
    dq_b = dq.astype(jnp.bfloat16).reshape(tokens, heads * head_dim)
    partial_value = contract_rows(dq_b, w_query)
    partial_value = partial_value + contract_rows(dk_mine.astype(jnp.bfloat16), w_key)
    partial_value = partial_value + contract_rows(dv_mine.astype(jnp.bfloat16), w_value)
    return lax.psum_scatter(
        partial_value.astype(jnp.bfloat16), "tp", scatter_dimension=1, tiled=True
    )


def solution(mesh):
    placed = (
        P("ctx", None),
        P(None, "tp"),
        P(None, "tp"),
        P(None, "tp"),
        P("ctx", "tp"),
        P("ctx", "tp"),
        P(),
    )
    return jax.shard_map(
        on_device, mesh=mesh, in_specs=placed, out_specs=P("ctx", "tp"), check_vma=False
    )
```

profile of v0, /device:TPU:2, one launch (start us, length us, event | category | flops | bytes accessed | tf_op | source)
XLA Modules:
  0.0 588.8 jit_solution(3103527456440463668)
XLA Ops:
  13.6 4.6 fusion.47
  19.2 70.6 %all-gather.3.cloned.1.call-done = bf16[8192,128]{1,0:T(8,128)(2,1)} async-done(((bf16[128,128]{1,0:T(8,128)(2,1)}), bf16[8192,128]{1,0:T(8,128)(2,1)}) %all-gather.3.cloned.1.call-update) | async-done | bytes 2097168 | tf_op jit(solution)/shard_map/all_gather | solution.py:98
  89.7 42.9 %while.36 = (s32[]{:T(128)}, f32[8,128]{1,0:T(8,128)S(1)}, f32[8,128]{1,0:T(8,128)S(1)}, s32[128]{0:T(128)S(1)}, s32[]{:T(128)}, /*index=5*/s32[128]{0:T(128)S(1...) while((s32[]{:T(128)}, f32[8,128]{1,0:T(8,128)S(1)}, ...), condition=%wide.region_9.10_spmd, body=%wide.region_2.9_spmd.sunk | while | flops 277381120 | bytes 9385225 | solution.py:108
  92.1 3.0 conditional.4
  97.4 3.0 conditional.4
  102.8 3.0 conditional.4
  108.1 3.0 conditional.4
  118.9 3.0 conditional.4
  124.2 3.0 conditional.4
  129.6 3.0 conditional.4
  132.6 34.9 %all-gather.5.cloned.1.call-done = bf16[8192,128]{1,0:T(8,128)(2,1)} async-done(((bf16[128,128]{1,0:T(8,128)(2,1)}), bf16[8192,128]{1,0:T(8,128)(2,1)}) %all-gather.5.cloned.1.call-update) | async-done | bytes 2097168 | tf_op jit(solution)/shard_map/all_gather | solution.py:99
  172.0 92.8 %while.37 = (s32[]{:T(128)}, f32[128,8,128]{2,0,1:T(8,128)S(1)}, f32[8192,128]{1,0:T(8,128)}, f32[8192,128]{1,0:T(8,128)}, s32[128]{0:T(128)S(1)}, /*index=5*/s3...) while((s32[]{:T(128)}, f32[128,8,128]{2,0,1:T(8,128)S(1)}, ...), condition=%wide.region_16.17_spmd, body=%wide.region_11.16_spmd.sunk | while | flops 1354397696 | bytes 23238016 | solution.py:119
  174.4 9.2 %conditional.5 = ((f32[128,8,128]{2,0,1:T(8,128)S(1)}, f32[8192,128]{1,0:T(8,128)}, f32[8192,128]{1,0:T(8,128)})) conditional(s32[]{:T(128)} %convert_element_type.94, (s32[1024]{0:T(1024)S(1)}, s32[128]{0:T(128)S(1)}, s32[]{:T(128)}, bf16[8192,128]{1,0:T(8,128)(2,1)}, bf16[128,8,128]{2,0,1:T(8,128)(2,1)S(1)}, /*index=5*/f32[8,128]{1,0:T(8,128)S(1)}, ...), branch_computations={%region_14.14_spmd, %region_15.15_spmd} | conditional | flops 1353973760 | bytes 23216726 | solution.py:50
  185.9 9.3 %conditional.5 = ((f32[128,8,128]{2,0,1:T(8,128)S(1)}, f32[8192,128]{1,0:T(8,128)}, f32[8192,128]{1,0:T(8,128)})) conditional(s32[]{:T(128)} %convert_element_type.94, (s32[1024]{0:T(1024)S(1)}, s32[128]{0:T(128)S(1)}, s32[]{:T(128)}, bf16[8192,128]{1,0:T(8,128)(2,1)}, bf16[128,8,128]{2,0,1:T(8,128)(2,1)S(1)}, /*index=5*/f32[8,128]{1,0:T(8,128)S(1)}, ...), branch_computations={%region_14.14_spmd, %region_15.15_spmd} | conditional | flops 1353973760 | bytes 23216726 | solution.py:50
  197.5 9.3 %conditional.5 = ((f32[128,8,128]{2,0,1:T(8,128)S(1)}, f32[8192,128]{1,0:T(8,128)}, f32[8192,128]{1,0:T(8,128)})) conditional(s32[]{:T(128)} %convert_element_type.94, (s32[1024]{0:T(1024)S(1)}, s32[128]{0:T(128)S(1)}, s32[]{:T(128)}, bf16[8192,128]{1,0:T(8,128)(2,1)}, bf16[128,8,128]{2,0,1:T(8,128)(2,1)S(1)}, /*index=5*/f32[8,128]{1,0:T(8,128)S(1)}, ...), branch_computations={%region_14.14_spmd, %region_15.15_spmd} | conditional | flops 1353973760 | bytes 23216726 | solution.py:50
  209.1 9.3 %conditional.5 = ((f32[128,8,128]{2,0,1:T(8,128)S(1)}, f32[8192,128]{1,0:T(8,128)}, f32[8192,128]{1,0:T(8,128)})) conditional(s32[]{:T(128)} %convert_element_type.94, (s32[1024]{0:T(1024)S(1)}, s32[128]{0:T(128)S(1)}, s32[]{:T(128)}, bf16[8192,128]{1,0:T(8,128)(2,1)}, bf16[128,8,128]{2,0,1:T(8,128)(2,1)S(1)}, /*index=5*/f32[8,128]{1,0:T(8,128)S(1)}, ...), branch_computations={%region_14.14_spmd, %region_15.15_spmd} | conditional | flops 1353973760 | bytes 23216726 | solution.py:50
  220.8 9.3 %conditional.5 = ((f32[128,8,128]{2,0,1:T(8,128)S(1)}, f32[8192,128]{1,0:T(8,128)}, f32[8192,128]{1,0:T(8,128)})) conditional(s32[]{:T(128)} %convert_element_type.94, (s32[1024]{0:T(1024)S(1)}, s32[128]{0:T(128)S(1)}, s32[]{:T(128)}, bf16[8192,128]{1,0:T(8,128)(2,1)}, bf16[128,8,128]{2,0,1:T(8,128)(2,1)S(1)}, /*index=5*/f32[8,128]{1,0:T(8,128)S(1)}, ...), branch_computations={%region_14.14_spmd, %region_15.15_spmd} | conditional | flops 1353973760 | bytes 23216726 | solution.py:50
  232.3 9.3 %conditional.5 = ((f32[128,8,128]{2,0,1:T(8,128)S(1)}, f32[8192,128]{1,0:T(8,128)}, f32[8192,128]{1,0:T(8,128)})) conditional(s32[]{:T(128)} %convert_element_type.94, (s32[1024]{0:T(1024)S(1)}, s32[128]{0:T(128)S(1)}, s32[]{:T(128)}, bf16[8192,128]{1,0:T(8,128)(2,1)}, bf16[128,8,128]{2,0,1:T(8,128)(2,1)S(1)}, /*index=5*/f32[8,128]{1,0:T(8,128)S(1)}, ...), branch_computations={%region_14.14_spmd, %region_15.15_spmd} | conditional | flops 1353973760 | bytes 23216726 | solution.py:50
  244.0 9.2 %conditional.5 = ((f32[128,8,128]{2,0,1:T(8,128)S(1)}, f32[8192,128]{1,0:T(8,128)}, f32[8192,128]{1,0:T(8,128)})) conditional(s32[]{:T(128)} %convert_element_type.94, (s32[1024]{0:T(1024)S(1)}, s32[128]{0:T(128)S(1)}, s32[]{:T(128)}, bf16[8192,128]{1,0:T(8,128)(2,1)}, bf16[128,8,128]{2,0,1:T(8,128)(2,1)S(1)}, /*index=5*/f32[8,128]{1,0:T(8,128)S(1)}, ...), branch_computations={%region_14.14_spmd, %region_15.15_spmd} | conditional | flops 1353973760 | bytes 23216726 | solution.py:50
  255.5 9.3 %conditional.5 = ((f32[128,8,128]{2,0,1:T(8,128)S(1)}, f32[8192,128]{1,0:T(8,128)}, f32[8192,128]{1,0:T(8,128)})) conditional(s32[]{:T(128)} %convert_element_type.94, (s32[1024]{0:T(1024)S(1)}, s32[128]{0:T(128)S(1)}, s32[]{:T(128)}, bf16[8192,128]{1,0:T(8,128)(2,1)}, bf16[128,8,128]{2,0,1:T(8,128)(2,1)S(1)}, /*index=5*/f32[8,128]{1,0:T(8,128)S(1)}, ...), branch_computations={%region_14.14_spmd, %region_15.15_spmd} | conditional | flops 1353973760 | bytes 23216726 | solution.py:50
  265.8 7.7 %fusion.58 = f32[128,4096]{1,0:T(8,128)} fusion(bf16[128,1024]{0,1:T(8,128)(2,1)S(1)} %bitcast.85, bf16[4096,1024]{1,0:T(8,128)(2,1)} %param.16), kind=kOutput, calls=%fused_computation.93 | convolution fusion | flops 1073741824 | bytes 10747904 | tf_op jit(solution)/shard_map/dot_general | solution.py:21
  273.5 133.5 %reduce-scatter.4.cloned.1.call-done = f32[128,128]{1,0:T(8,128)} async-done(((f32[8192,128]{1,0:T(8,128)}), f32[128,128]{1,0:T(8,128)}) %reduce-scatter.4.cloned.1.call-update) | async-done | bytes 65552 | tf_op jit(solution)/shard_map/reduce_scatter | solution.py:121
  409.1 144.7 %reduce-scatter.6.cloned.1.call-done = f32[128,128]{1,0:T(8,128)} async-done(((f32[8192,128]{1,0:T(8,128)}), f32[128,128]{1,0:T(8,128)}) %reduce-scatter.6.cloned.1.call-update) | async-done | bytes 65552 | tf_op jit(solution)/shard_map/reduce_scatter | solution.py:122
  556.5 25.7 %reduce-scatter.8.cloned.1.call-done = bf16[128,1024]{1,0:T(8,128)(2,1)} async-done(((bf16[128,4096]{1,0:T(8,128)(2,1)}), bf16[128,1024]{1,0:T(8,128)(2,1)}) %reduce-scatter.8.cloned.1.call-update) | async-done | bytes 262160 | tf_op jit(solution)/shard_map/reduce_scatter | solution.py:128
  (184 shorter events, 135.7 us)
Async XLA Ops:
  6.5 1.4 copy-start
  6.5 7.0 %copy-start.1 = (bf16[128,4096]{1,0:T(8,128)(2,1)S(1)}, bf16[128,4096]{1,0:T(8,128)(2,1)}, u32[]{:S(2)}) copy-start(bf16[128,4096]{1,0:T(8,128)(2,1)} %param.15) | copy-start | bytes 3145732
  6.5 6.4 %copy-start.2 = (bf16[128,1024]{1,0:T(8,128)(2,1)S(1)}, bf16[128,1024]{1,0:T(8,128)(2,1)}, u32[]{:S(2)}) copy-start(bf16[128,1024]{1,0:T(8,128)(2,1)} %param.20) | copy-start | bytes 786436
  6.5 6.8 %copy-start.3 = (bf16[128,1024]{1,0:T(8,128)(2,1)S(1)}, bf16[128,1024]{1,0:T(8,128)(2,1)}, u32[]{:S(2)}) copy-start(bf16[128,1024]{1,0:T(8,128)(2,1)} %param.19) | copy-start | bytes 786436
  6.5 83.2 %all-gather.3.cloned.1.call-start = ((), (), s32[]{:S(2)}) async-start(), calls=%async_computation.3 | async-start | bytes 2129920 | tf_op jit(solution)/shard_map/all_gather | solution.py:98
  10.2 157.4 %all-gather.5.cloned.1.call-start = ((), (), s32[]{:S(2)}) async-start(), calls=%async_computation.4 | async-start | bytes 2129920 | tf_op jit(solution)/shard_map/all_gather | solution.py:99
  12.8 394.2 %reduce-scatter.4.cloned.1.call-start = ((), (), s32[]{:S(2)}) async-start(), calls=%async_computation.5 | async-start | bytes 4259840 | tf_op jit(solution)/shard_map/reduce_scatter | solution.py:121
  13.6 4.7 copy-start.4
  264.8 289.0 %reduce-scatter.6.cloned.1.call-start = ((), (), s32[]{:S(2)}) async-start(), calls=%async_computation.6 | async-start | bytes 4259840 | tf_op jit(solution)/shard_map/reduce_scatter | solution.py:122
  265.4 316.9 %reduce-scatter.8.cloned.1.call-start = ((), (), s32[]{:S(2)}) async-start(), calls=%async_computation.7 | async-start | bytes 1310720 | tf_op jit(solution)/shard_map/reduce_scatter | solution.py:128
Sparse Core Ops, SparseCore 0:
  10.3 79.3 all-gather.2
  92.5 75.0 all-gather.4
  264.9 142.0 reduce-scatter.3
  411.0 142.7 reduce-scatter.5
  556.7 25.5 reduce-scatter.7
where the time goes:
time: 590 us; the launch traced here: 589 us
  waiting for transfers between devices  410 us (69%)
  matrix products  108 us (18%)
  other arithmetic  29.7 us (5%)
  loops' own time  21 us (4%)
  between operations  13.3 us (2%)
  local copies, waits for them, and re-layouts  6.58 us (1%)
    reduce_scatter x1, waiting for transfers between devices, on_device(): lax.psum_scatter(dv_full, 'ctx', scatter_dimension=0, tiled=True)  145 us
    reduce_scatter x1, waiting for transfers between devices, on_device(): lax.psum_scatter(dk_full, 'ctx', scatter_dimension=0, tiled=True)  134 us
    all_gather x1, waiting for transfers between devices, on_device(): lax.all_gather(keys, 'ctx', axis=0, tiled=True)  70.6 us
    all_gather x1, waiting for transfers between devices, on_device(): lax.all_gather(values, 'ctx', axis=0, tiled=True)  34.9 us
    dot_general x16, matrix products, work(): jnp.einsum('thd,nd->htn', queries, piece_k, preferred_element_type=jnp.fl...  26.9 us
    reduce_scatter x1, waiting for transfers between devices, on_device(): lax.psum_scatter(partial_value.astype(jnp.bfloat16), 'tp', scatter_dimens...  25.7 us
    dot_general x8, matrix products, work(): jnp.einsum('thd,nd->htn', grads3, piece_v, preferred_element_type=jnp.flo...  19.7 us
    dot_general x8, matrix products, work(): jnp.einsum('htn,nd->thd', ds_b, piece_k, preferred_element_type=jnp.float32)  13.9 us
  transfers between devices with their start and end apart: 5, of which 5 were waited for; matrix products, arithmetic and copies ran while one was open for 9% of the time, Pallas kernels for 0%

commit v1 on v0

--- a/solution.py
+++ b/solution.py
@@ -5,6 +5,13 @@
 from jax.sharding import PartitionSpec as P
 
 big_negative = -1e30
+
+
+def direct_teams_over_axis(xin):
+    return jnp.concatenate(
+        lax.all_to_all(jnp.stack([xin for _ in range(lax.axis_size("ctx"))], axis=0), "ctx", 0, 0),
+        axis=0,
+    )
 
 
 def row_positions(order, start, count, span):
@@ -95,7 +102,7 @@
     zero_rows = jnp.zeros((seq, head_dim), jnp.float32)
     grad_init = (jnp.zeros((tokens, heads, head_dim), jnp.float32), zero_rows, zero_rows)
     all_keys, all_values = (
-        lax.all_gather(keys, "ctx", axis=0, tiled=True),
+        direct_teams_over_axis(keys),
         lax.all_gather(values, "ctx", axis=0, tiled=True),
     )
     block = math.gcd(seq, 1024)

time: 590 us -> 534 us (0.905)
  waiting for transfers between devices: 410 us -> 342 us
  starting transfers between devices: 0.38 us -> 12.4 us
  matrix products: 108 us -> 100 us
  local copies, waits for them, and re-layouts: 6.58 us -> 12.8 us
    all_gather x1 -> x0, waiting for transfers between devices: 70.6 us -> none  [on_device(): lax.all_gather(keys, 'ctx', axis=0, tiled=True)]
    all_to_all x0 -> x1, waiting for transfers between devices: none -> 37 us  [direct_teams_over_axis(): lax.all_to_all(jnp.stack([xin for _ in range(lax.axis_size('ctx'))], axis...]
    all_gather x1, waiting for transfers between devices: 34.9 us -> 0.02 us  [on_device(): lax.all_gather(values, 'ctx', axis=0, tiled=True)]
    all_to_all x0 -> x1, starting transfers between devices: none -> 12 us  [direct_teams_over_axis(): lax.all_to_all(jnp.stack([xin for _ in range(lax.axis_size('ctx'))], axis...]
    dot_general x16, matrix products: 26.9 us -> 19.3 us  [work(): jnp.einsum('thd,nd->htn', queries, piece_k, preferred_element_type=jnp.fl...]
  transfers between devices with their start and end apart: 5 -> 5, of which waited for: 5 -> 4; matrix products, arithmetic and copies ran while one was open for 9% -> 9% of each run, Pallas kernels for 0% -> 0%
where the time goes in v1:
time: 534 us; the launch traced here: 532 us
  waiting for transfers between devices  342 us (64%)
  matrix products  100 us (19%)
  other arithmetic  30.7 us (6%)
  loops' own time  21.3 us (4%)
  between operations  13.3 us (2%)
  local copies, waits for them, and re-layouts  12.8 us (2%)
  starting transfers between devices  12.4 us (2%)
    reduce_scatter x1, waiting for transfers between devices, on_device(): lax.psum_scatter(dv_full, 'ctx', scatter_dimension=0, tiled=True)  145 us
    reduce_scatter x1, waiting for transfers between devices, on_device(): lax.psum_scatter(dk_full, 'ctx', scatter_dimension=0, tiled=True)  134 us
    all_to_all x1, waiting for transfers between devices, direct_teams_over_axis(): lax.all_to_all(jnp.stack([xin for _ in range(lax.axis_size('ctx'))], axis...  37 us
    reduce_scatter x1, waiting for transfers between devices, on_device(): lax.psum_scatter(partial_value.astype(jnp.bfloat16), 'tp', scatter_dimens...  25.8 us
    dot_general x8, matrix products, work(): jnp.einsum('thd,nd->htn', grads3, piece_v, preferred_element_type=jnp.flo...  19.7 us
    dot_general x16, matrix products, work(): jnp.einsum('thd,nd->htn', queries, piece_k, preferred_element_type=jnp.fl...  19.3 us
    dot_general x8, matrix products, work(): jnp.einsum('htn,nd->thd', ds_b, piece_k, preferred_element_type=jnp.float32)  13.9 us
    dot_general x8, matrix products, work(): jnp.einsum('htn,thd->nd', p_b, grads3, preferred_element_type=jnp.float32)  13.3 us
  transfers between devices with their start and end apart: 5, of which 4 were waited for; matrix products, arithmetic and copies ran while one was open for 9% of the time, Pallas kernels for 0%

profile of v1, /device:TPU:2, one launch (start us, length us, event | category | flops | bytes accessed | tf_op | source)
XLA Modules:
  0.0 532.3 jit_solution(16171737559414458763)
XLA Ops:
  11.3 12.0 %all-to-all-start = ((bf16[64,128,128]{2,1,0:T(8,128)(2,1)}), bf16[64,128,128]{2,1,0:T(8,128)(2,1)S(1)}, u32[]{:S(2)}, u32[]{:S(2)}) async-start(bf16[64,128,128]{2,1,0:T(8,128)(2,1)} %stack.2), calls=%async_computation | async-start | bytes 4194304 | tf_op jit(solution)/shard_map/all_to_all | solution.py:12
  23.4 2.6 convolution_convert_fusion.1
  29.8 5.0 fusion.47
  36.8 37.0 %all-to-all-done = bf16[64,128,128]{2,1,0:T(8,128)(2,1)S(1)} async-done(((bf16[64,128,128]{2,1,0:T(8,128)(2,1)}), bf16[64,128,128]{2,1,0:T(8,128)(2,1)S(1)}, u32[]{:S(2)}, u32[]{:S(2)}) %all-to-all-start) | async-done | bytes 2097184 | tf_op jit(solution)/shard_map/all_to_all | solution.py:12
  73.8 35.5 %while.36 = (s32[]{:T(128)}, f32[8,128]{1,0:T(8,128)S(1)}, f32[8,128]{1,0:T(8,128)S(1)}, s32[128]{0:T(128)S(1)}, s32[]{:T(128)}, /*index=5*/s32[128]{0:T(128)S(1...) while((s32[]{:T(128)}, f32[8,128]{1,0:T(8,128)S(1)}, ...), condition=%wide.region_9.10_spmd, body=%wide.region_2.9_spmd.sunk | while | flops 277381120 | bytes 9385225 | solution.py:115
  115.2 92.8 %while.37 = (s32[]{:T(128)}, f32[128,8,128]{2,0,1:T(8,128)S(1)}, f32[8192,128]{1,0:T(8,128)}, f32[8192,128]{1,0:T(8,128)}, s32[128]{0:T(128)S(1)}, /*index=5*/s3...) while((s32[]{:T(128)}, f32[128,8,128]{2,0,1:T(8,128)S(1)}, ...), condition=%wide.region_16.17_spmd, body=%wide.region_11.16_spmd.sunk | while | flops 1354397696 | bytes 23238016 | solution.py:126
  117.5 9.3 %conditional.5 = ((f32[128,8,128]{2,0,1:T(8,128)S(1)}, f32[8192,128]{1,0:T(8,128)}, f32[8192,128]{1,0:T(8,128)})) conditional(s32[]{:T(128)} %convert_element_type.94, (s32[1024]{0:T(1024)S(1)}, s32[128]{0:T(128)S(1)}, s32[]{:T(128)}, bf16[8192,128]{1,0:T(8,128)(2,1)}, bf16[128,8,128]{2,0,1:T(8,128)(2,1)S(1)}, /*index=5*/f32[8,128]{1,0:T(8,128)S(1)}, ...), branch_computations={%region_14.14_spmd, %region_15.15_spmd} | conditional | flops 1353973760 | bytes 23216726 | solution.py:57
  129.1 9.3 %conditional.5 = ((f32[128,8,128]{2,0,1:T(8,128)S(1)}, f32[8192,128]{1,0:T(8,128)}, f32[8192,128]{1,0:T(8,128)})) conditional(s32[]{:T(128)} %convert_element_type.94, (s32[1024]{0:T(1024)S(1)}, s32[128]{0:T(128)S(1)}, s32[]{:T(128)}, bf16[8192,128]{1,0:T(8,128)(2,1)}, bf16[128,8,128]{2,0,1:T(8,128)(2,1)S(1)}, /*index=5*/f32[8,128]{1,0:T(8,128)S(1)}, ...), branch_computations={%region_14.14_spmd, %region_15.15_spmd} | conditional | flops 1353973760 | bytes 23216726 | solution.py:57
  140.7 9.3 %conditional.5 = ((f32[128,8,128]{2,0,1:T(8,128)S(1)}, f32[8192,128]{1,0:T(8,128)}, f32[8192,128]{1,0:T(8,128)})) conditional(s32[]{:T(128)} %convert_element_type.94, (s32[1024]{0:T(1024)S(1)}, s32[128]{0:T(128)S(1)}, s32[]{:T(128)}, bf16[8192,128]{1,0:T(8,128)(2,1)}, bf16[128,8,128]{2,0,1:T(8,128)(2,1)S(1)}, /*index=5*/f32[8,128]{1,0:T(8,128)S(1)}, ...), branch_computations={%region_14.14_spmd, %region_15.15_spmd} | conditional | flops 1353973760 | bytes 23216726 | solution.py:57
  142.6 2.5 fusion.13
  152.3 9.3 %conditional.5 = ((f32[128,8,128]{2,0,1:T(8,128)S(1)}, f32[8192,128]{1,0:T(8,128)}, f32[8192,128]{1,0:T(8,128)})) conditional(s32[]{:T(128)} %convert_element_type.94, (s32[1024]{0:T(1024)S(1)}, s32[128]{0:T(128)S(1)}, s32[]{:T(128)}, bf16[8192,128]{1,0:T(8,128)(2,1)}, bf16[128,8,128]{2,0,1:T(8,128)(2,1)S(1)}, /*index=5*/f32[8,128]{1,0:T(8,128)S(1)}, ...), branch_computations={%region_14.14_spmd, %region_15.15_spmd} | conditional | flops 1353973760 | bytes 23216726 | solution.py:57
  154.2 2.5 fusion.13
  163.9 9.3 %conditional.5 = ((f32[128,8,128]{2,0,1:T(8,128)S(1)}, f32[8192,128]{1,0:T(8,128)}, f32[8192,128]{1,0:T(8,128)})) conditional(s32[]{:T(128)} %convert_element_type.94, (s32[1024]{0:T(1024)S(1)}, s32[128]{0:T(128)S(1)}, s32[]{:T(128)}, bf16[8192,128]{1,0:T(8,128)(2,1)}, bf16[128,8,128]{2,0,1:T(8,128)(2,1)S(1)}, /*index=5*/f32[8,128]{1,0:T(8,128)S(1)}, ...), branch_computations={%region_14.14_spmd, %region_15.15_spmd} | conditional | flops 1353973760 | bytes 23216726 | solution.py:57
  165.8 2.5 fusion.13
  175.5 9.3 %conditional.5 = ((f32[128,8,128]{2,0,1:T(8,128)S(1)}, f32[8192,128]{1,0:T(8,128)}, f32[8192,128]{1,0:T(8,128)})) conditional(s32[]{:T(128)} %convert_element_type.94, (s32[1024]{0:T(1024)S(1)}, s32[128]{0:T(128)S(1)}, s32[]{:T(128)}, bf16[8192,128]{1,0:T(8,128)(2,1)}, bf16[128,8,128]{2,0,1:T(8,128)(2,1)S(1)}, /*index=5*/f32[8,128]{1,0:T(8,128)S(1)}, ...), branch_computations={%region_14.14_spmd, %region_15.15_spmd} | conditional | flops 1353973760 | bytes 23216726 | solution.py:57
  187.1 9.2 %conditional.5 = ((f32[128,8,128]{2,0,1:T(8,128)S(1)}, f32[8192,128]{1,0:T(8,128)}, f32[8192,128]{1,0:T(8,128)})) conditional(s32[]{:T(128)} %convert_element_type.94, (s32[1024]{0:T(1024)S(1)}, s32[128]{0:T(128)S(1)}, s32[]{:T(128)}, bf16[8192,128]{1,0:T(8,128)(2,1)}, bf16[128,8,128]{2,0,1:T(8,128)(2,1)S(1)}, /*index=5*/f32[8,128]{1,0:T(8,128)S(1)}, ...), branch_computations={%region_14.14_spmd, %region_15.15_spmd} | conditional | flops 1353973760 | bytes 23216726 | solution.py:57
  189.0 2.5 fusion.13
  198.7 9.3 %conditional.5 = ((f32[128,8,128]{2,0,1:T(8,128)S(1)}, f32[8192,128]{1,0:T(8,128)}, f32[8192,128]{1,0:T(8,128)})) conditional(s32[]{:T(128)} %convert_element_type.94, (s32[1024]{0:T(1024)S(1)}, s32[128]{0:T(128)S(1)}, s32[]{:T(128)}, bf16[8192,128]{1,0:T(8,128)(2,1)}, bf16[128,8,128]{2,0,1:T(8,128)(2,1)S(1)}, /*index=5*/f32[8,128]{1,0:T(8,128)S(1)}, ...), branch_computations={%region_14.14_spmd, %region_15.15_spmd} | conditional | flops 1353973760 | bytes 23216726 | solution.py:57
  200.6 2.5 fusion.13
  209.0 7.7 %fusion.58 = f32[128,4096]{1,0:T(8,128)} fusion(bf16[128,1024]{0,1:T(8,128)(2,1)S(1)} %bitcast.87, bf16[4096,1024]{1,0:T(8,128)(2,1)} %param.16), kind=kOutput, calls=%fused_computation.93 | convolution fusion | flops 1073741824 | bytes 10747904 | tf_op jit(solution)/shard_map/dot_general | solution.py:28
  216.7 133.7 %reduce-scatter.4.cloned.1.call-done = f32[128,128]{1,0:T(8,128)} async-done(((f32[8192,128]{1,0:T(8,128)}), f32[128,128]{1,0:T(8,128)}) %reduce-scatter.4.cloned.1.call-update) | async-done | bytes 65552 | tf_op jit(solution)/shard_map/reduce_scatter | solution.py:128
  352.4 144.8 %reduce-scatter.6.cloned.1.call-done = f32[128,128]{1,0:T(8,128)} async-done(((f32[8192,128]{1,0:T(8,128)}), f32[128,128]{1,0:T(8,128)}) %reduce-scatter.6.cloned.1.call-update) | async-done | bytes 65552 | tf_op jit(solution)/shard_map/reduce_scatter | solution.py:129
  497.3 2.7 fusion.46
  500.0 25.8 %reduce-scatter.8.cloned.1.call-done = bf16[128,1024]{1,0:T(8,128)(2,1)} async-done(((bf16[128,4096]{1,0:T(8,128)(2,1)}), bf16[128,1024]{1,0:T(8,128)(2,1)}) %reduce-scatter.8.cloned.1.call-update) | async-done | bytes 262160 | tf_op jit(solution)/shard_map/reduce_scatter | solution.py:135
  (184 shorter events, 130.5 us)
Async XLA Ops:
  6.5 1.2 copy-start
  11.3 62.6 %all-to-all-start = ((bf16[64,128,128]{2,1,0:T(8,128)(2,1)}), bf16[64,128,128]{2,1,0:T(8,128)(2,1)S(1)}, u32[]{:S(2)}, u32[]{:S(2)}) async-start(bf16[64,128,128]{2,1,0:T(8,128)(2,1)} %stack.2), calls=%async_computation | async-start | bytes 4194304 | tf_op jit(solution)/shard_map/all_to_all | solution.py:12
  23.3 86.1 %all-gather.2.cloned.1.call-start = ((), (), s32[]{:S(2)}) async-start(), calls=%async_computation.4 | async-start | bytes 2129920 | tf_op jit(solution)/shard_map/all_gather | solution.py:106
  25.9 324.4 %reduce-scatter.4.cloned.1.call-start = ((), (), s32[]{:S(2)}) async-start(), calls=%async_computation.5 | async-start | bytes 4259840 | tf_op jit(solution)/shard_map/reduce_scatter | solution.py:128
  27.1 2.7 copy-start.2
  29.8 5.1 copy-start.4
  109.4 1.3 copy-start.1
  110.7 4.5 copy-start.3
  208.0 289.2 %reduce-scatter.6.cloned.1.call-start = ((), (), s32[]{:S(2)}) async-start(), calls=%async_computation.6 | async-start | bytes 4259840 | tf_op jit(solution)/shard_map/reduce_scatter | solution.py:129
  208.8 317.0 %reduce-scatter.8.cloned.1.call-start = ((), (), s32[]{:S(2)}) async-start(), calls=%async_computation.7 | async-start | bytes 1310720 | tf_op jit(solution)/shard_map/reduce_scatter | solution.py:135
Sparse Core Ops, SparseCore 0:
  26.9 79.6 all-gather.1
  208.1 142.1 reduce-scatter.3
  354.5 142.7 reduce-scatter.5
  500.1 25.5 reduce-scatter.7
